TPU v7x, 128 devices: a whole 4x4x4 slice. The times are simulated.
128 devices in a mesh: prow: 8 (over x, core), pcol: 16 (over y, z).
Axes of the slice: x: 4, y: 4, z: 4, core: 2. Of those that a mesh axis runs over, the one named last changes fastest.
Arguments:
- basis: bfloat16 [512, 256], replicated, may hold values from -0.25 to 0.25
- potentials: float32 [8, 512], replicated, may hold values from -6 to 6
- orbitals: bfloat16 [64, 512], P('pcol'), may hold values from -6 to 6
- chan_orbital: int32 [256], replicated, may hold values from 0 to 63
- pair_list: int32 [24576, 3], P(('prow', 'pcol')), may hold values from 0 to 255, as said below
- slot_list: int32 [24576], P(('prow', 'pcol')), may hold values from 0 to 255
- coefs: float32 [24576, 2], P(('prow', 'pcol')), may hold values from -6 to 6
- exchange_ops: bfloat16 [24576, 128, 256], P(('prow', 'pcol')), may hold values from -1.1953125 to 1.1953125
Outputs:
- hamiltonian: bfloat16 [32, 8, 2, 16, 256, 256], P(None, 'prow', None, 'pcol')
Inputs may be any that keep to these rules, and one draw needn't show every extreme that they name: `pair_list`: columns 0 and 1 are channels a, b; column 2 is a multipole order below 8. (b // 16 - a // 16) modulo 256 // 16 is below 2. Terms of one device with the same slot s have the same two channels, and the block (a, b) belongs to owner s // 2 in prow-major order: a % 8 and b % 16 are that owner's prow and pcol indices.
All inputs are finite; a program needn't handle non-finite values.
Results may differ from a plain program's by a relative error of at most 0.0058.
Values may be sent and summed in bfloat16 or wider, within the bound.
No kernel may reach another device: no remote copies, remote signals or barrier semaphores. Data moves between devices by JAX's collectives and lax.ppermute only.
A program may use at most 320 MiB of HBM per device.

v0:
```python
import jax
import jax.numpy as jnp
from jax import lax
from jax.sharding import PartitionSpec as P

CAP = 2
BAND = 2
RBLK = 32


def build_tiles(weights_group, exchange_group, basis):
    weights_group = lax.optimization_barrier(weights_group)
    scaled = (
        weights_group.astype(jnp.float32)[:, :, None] * basis.astype(jnp.float32)[None]
    ).astype(jnp.bfloat16)
    inner_rows = basis[: exchange_group.shape[1]]
    local_part = jnp.einsum("qa,gqb->gab", basis, scaled, preferred_element_type=jnp.float32)
    exchange_part = jnp.einsum(
        "qa,gqb->gab", inner_rows, exchange_group, preferred_element_type=jnp.float32
    )
    return (local_part + exchange_part).astype(jnp.bfloat16)


def sum_blocks(built_tiles, idents, block_count):
    select = (jnp.arange(block_count, dtype=jnp.int32)[:, None] == idents[None, :]).astype(
        jnp.bfloat16
    )
    spline_width = built_tiles.shape[1]
    summed = jnp.dot(
        select,
        built_tiles.reshape(built_tiles.shape[0], spline_width * spline_width),
        preferred_element_type=jnp.float32,
    )
    return summed.reshape(block_count, spline_width, spline_width)


def on_device(basis, potentials, orbitals, chan_orbital, pair_list, slot_list, coefs, exchange_ops):
    all_orbitals = lax.all_gather(orbitals, "pcol", axis=0, tiled=True)
    row_devs = lax.axis_size("prow")
    col_devs = lax.axis_size("pcol")
    slot_count = row_devs * col_devs * CAP
    chan_count = chan_orbital.shape[0]
    orb_count = all_orbitals.shape[0]
    point_count = basis.shape[0]
    spline_count = basis.shape[1]
    inner_count = exchange_ops.shape[1]
    term_count = exchange_ops.shape[0]
    col_groups = chan_count // col_devs
    block_count = RBLK * BAND
    first_chan = pair_list[:, 0]
    second_chan = pair_list[:, 1]
    multipole = pair_list[:, 2]
    channels = jnp.arange(chan_count, dtype=jnp.int32)
    orb_ids = jnp.arange(orb_count, dtype=jnp.int32)
    first_orb = jnp.sum(
        jnp.where(first_chan[:, None] == channels[None, :], chan_orbital[None, :], 0), axis=1
    )
    second_orb = jnp.sum(
        jnp.where(second_chan[:, None] == channels[None, :], chan_orbital[None, :], 0), axis=1
    )
    first_rows = jnp.dot(
        (first_orb[:, None] == orb_ids[None, :]).astype(jnp.bfloat16),
        all_orbitals,
        preferred_element_type=jnp.float32,
    )
    second_rows = jnp.dot(
        (second_orb[:, None] == orb_ids[None, :]).astype(jnp.bfloat16),
        all_orbitals,
        preferred_element_type=jnp.float32,
    )
    pick_pot = (
        multipole[:, None] == jnp.arange(potentials.shape[0], dtype=jnp.int32)[None, :]
    ).astype(jnp.float32)
    pot_rows = jnp.dot(pick_pot, potentials, precision=lax.Precision.HIGHEST)
    radial = coefs[:, 0:1] * pot_rows + coefs[:, 1:2] * (first_rows * second_rows)
    matches = slot_list[None, :] == jnp.arange(slot_count, dtype=jnp.int32)[:, None]
    slot_weight = jnp.dot(
        matches.astype(jnp.float32), radial, precision=lax.Precision.HIGHEST
    ).astype(jnp.bfloat16)
    exchange_rows = exchange_ops.reshape(term_count, inner_count * spline_count)
    slot_exchange = jnp.dot(
        matches.astype(jnp.bfloat16), exchange_rows, preferred_element_type=jnp.float32
    ).astype(jnp.bfloat16)
    slot_exchange = slot_exchange.reshape(slot_count, inner_count, spline_count)
    offset = jnp.mod(second_chan // col_devs - first_chan // col_devs, col_groups)
    block_index = first_chan // row_devs * BAND + offset
    slot_ids = jnp.max(jnp.where(matches, block_index[None, :], -1), axis=1)
    built_tiles = lax.map(
        lambda slot_group: build_tiles(slot_group[0], slot_group[1], basis),
        (
            slot_weight.reshape(slot_count // 16, 16, point_count),
            slot_exchange.reshape(slot_count // 16, 16, inner_count, spline_count),
        ),
    )
    built_tiles = built_tiles.reshape(row_devs, col_devs, CAP, spline_count, spline_count)
    received, idents = (
        lax.all_to_all(
            lax.all_to_all(built_tiles, "prow", split_axis=0, concat_axis=0, tiled=True),
            "pcol",
            split_axis=1,
            concat_axis=1,
            tiled=True,
        ),
        lax.all_to_all(
            lax.all_to_all(
                slot_ids.reshape(row_devs, col_devs, CAP),
                "prow",
                split_axis=0,
                concat_axis=0,
                tiled=True,
            ),
            "pcol",
            split_axis=1,
            concat_axis=1,
            tiled=True,
        ),
    )
    blocks = sum_blocks(
        received.reshape(slot_count, spline_count, spline_count),
        idents.reshape(slot_count),
        block_count,
    )
    return blocks.astype(jnp.bfloat16).reshape(RBLK, 1, BAND, 1, spline_count, spline_count)


def solution(mesh):
    placed = (
        P(),
        P(),
        P("pcol", None),
        P(),
        P(("prow", "pcol"), None),
        P(("prow", "pcol")),
        P(("prow", "pcol"), None),
        P(("prow", "pcol"), None, None),
    )
    return jax.shard_map(
        on_device,
        mesh=mesh,
        in_specs=placed,
        out_specs=P(None, "prow", None, "pcol", None, None),
        check_vma=False,
    )
```

profile of v0, /device:TPU:80, one launch (start us, length us, event | category | flops | bytes accessed | tf_op | source)
XLA Modules:
  0.0 1376.1 jit_solution(16522838021894493454)
XLA Ops:
  2.5 4.3 all-to-all-start
  8.5 21.0 %all-gather = bf16[16,4,512]{2,1,0:T(4,128)(2,1)S(1)} all-gather(bf16[1,4,512]{2,1,0:T(4,128)(2,1)} %bitcast.71), channel_id=1, replica_groups=mesh['prow'=8,'pcol'=16] {'pcol'}, dimensions={0}, use_global_device_ids=true | all-gather | bytes 69632 | tf_op jit(solution)/shard_map/all_gather | solution.py:38
  31.6 13.9 %copy.50 = bf16[24,8,128,256]{3,1,2,0:T(8,128)(2,1)} copy(bf16[24,8,128,256]{3,2,1,0:T(8,128)(2,1)} %bitcast.62) | data formatting | bytes 25165824
  45.5 12.7 convolution_convert_fusion
  58.2 15.7 %copy.51 = bf16[32,8,128,256]{3,2,1,0:T(8,128)(2,1)} copy(bf16[32,8,128,256]{3,1,2,0:T(8,128)(2,1)} %bitcast.58) | data formatting | bytes 33554432
  73.9 144.8 %while.10 = (s32[]{:T(128)}, bf16[16,16,256,256]{3,2,1,0:T(8,128)(2,1)}, bf16[16,16,512]{2,1,0:T(8,128)(2,1)S(1)}, bf16[512,256]{1,0:T(8,128)(2,1)S(1)}, bf16[16,16,128,256]{3,2,1,0:T(8,128)(2,1)}, /*index=5*/s32[]{:T(128)}) while((s32[]{:T(128)}, bf16[16,16,256,256]{3,2,1,0:T(8,128)(2,1)}, bf16[16,16,512]{2,1,0:T(8,128)(2,1)S(1)}, ...), condition=%wide.region_4.5_spmd, body=%wide.region_3.4_spmd.sunk | while | flops 1348476928 | bytes 21676120 | solution.py:88
  75.3 3.3 fusion.40
  84.4 3.3 fusion.40
  102.5 3.3 fusion.40
  129.7 3.3 fusion.40
  147.7 3.3 fusion.40
  156.8 3.3 fusion.40
  184.0 3.3 fusion.40
  218.7 7.2 all-to-all-start.2
  226.6 363.6 %all-to-all-done.2 = bf16[8,16,2,256,256]{4,3,2,1,0:T(8,128)(2,1)} async-done(((bf16[8,16,2,256,256]{4,3,2,1,0:T(8,128)(2,1)}), bf16[8,16,2,256,256]{4,3,2,1,0:T(8,128)(2,1)}, u32[]{:S(2)}, u32[]{:S(2)}) %all-to-all-start.2) | async-done | bytes 33554464 | tf_op jit(solution)/shard_map/all_to_all | solution.py:98
  590.2 8.3 all-to-all-start.1
  598.5 23.0 %copy.42 = bf16[8,16,2,256,256]{4,3,2,0,1:T(8,128)(2,1)} copy(bf16[8,16,2,256,256]{4,3,2,1,0:T(8,128)(2,1)} %all-to-all-done.2) | data formatting | bytes 67108864 | tf_op jit(solution)/shard_map/all_to_all | solution.py:98
  621.4 7.2 all-to-all-start.3
  629.0 618.7 %all-to-all-done.3 = bf16[8,16,2,256,256]{4,3,2,0,1:T(8,128)(2,1)} async-done(((bf16[8,16,2,256,256]{4,3,2,0,1:T(8,128)(2,1)}), bf16[8,16,2,256,256]{4,3,2,0,1:T(8,128)(2,1)}, u32[]{:S(2)}, u32[]{:S(2)}) %all-to-all-start.3) | async-done | bytes 33554464 | tf_op jit(solution)/shard_map/all_to_all | solution.py:97
  1247.7 23.0 %copy.43 = bf16[8,16,2,256,256]{4,3,2,1,0:T(8,128)(2,1)} copy(bf16[8,16,2,256,256]{4,3,2,0,1:T(8,128)(2,1)} %all-to-all-done.3) | data formatting | bytes 67108864 | tf_op jit(solution)/shard_map/all_to_all | solution.py:97
  1270.7 31.0 %copy.52 = bf16[32,8,256,256]{3,1,2,0:T(8,128)(2,1)} copy(bf16[32,8,256,256]{3,2,1,0:T(8,128)(2,1)} %bitcast.56) | data formatting | bytes 67108864
  1301.7 44.0 %copy.44 = bf16[65536,256]{1,0:T(8,128)(2,1)} copy(bf16[65536,256]{0,1:T(8,128)(2,1)} %bitcast.57) | data formatting | bytes 67108864 | tf_op jit(solution)/shard_map/dot_general | solution.py:29
  1345.6 18.9 %convolution_convert_fusion.1 = bf16[64,256,256]{2,0,1:T(8,128)(2,1)} fusion(bf16[256,256,256]{2,1,0:T(8,128)(2,1)} %bitcast.55, s32[256]{0:T(256)S(1)} %eq.101), kind=kOutput, calls=%fused_computation.15 | convolution fusion | flops 2151694336 | bytes 41944064 | tf_op jit(solution)/shard_map/dot_general | solution.py:29
  1364.5 11.5 copy.46
  (131 shorter events, 128.5 us)
Async XLA Ops:
  0.0 30.0 %copy-start = (f32[8,512]{1,0:T(8,128)S(1)}, f32[8,512]{1,0:T(8,128)}, u32[]{:S(2)}) copy-start(f32[8,512]{1,0:T(8,128)} %param.11) | copy-start | bytes 49156
  0.0 45.5 %copy-start.3 = (s32[192]{0:T(256)S(1)}, s32[192]{0:T(256)}, u32[]{:S(2)}) copy-start(s32[192]{0:T(256)} %param.15) | copy-start | bytes 2308
  2.5 216.2 %all-to-all-start = ((s32[8,16,2]{1,2,0:T(2,128)}), s32[8,16,2]{1,2,0:T(2,128)S(1)}, u32[]{:S(2)}, u32[]{:S(2)}) async-start(s32[8,16,2]{1,2,0:T(2,128)} %copy.37), calls=%async_computation | async-start | bytes 16384 | tf_op jit(solution)/shard_map/all_to_all | solution.py:105
  58.2 15.7 %copy-start.2 = (bf16[512,256]{1,0:T(8,128)(2,1)S(1)}, bf16[512,256]{1,0:T(8,128)(2,1)}, u32[]{:S(2)}) copy-start(bf16[512,256]{1,0:T(8,128)(2,1)} %param.10) | copy-start | bytes 786436
  218.7 371.5 %all-to-all-start.2 = ((bf16[8,16,2,256,256]{4,3,2,1,0:T(8,128)(2,1)}), bf16[8,16,2,256,256]{4,3,2,1,0:T(8,128)(2,1)}, u32[]{:S(2)}, u32[]{:S(2)}) async-start(bf16[8,16,2,256,256]{4,3,2,1,0:T(8,128)(2,1)} %bitcast.60), calls=%async_computation.2 | async-start | bytes 67108864 | tf_op jit(solution)/shard_map/all_to_all | solution.py:98
  590.2 31.2 %all-to-all-start.1 = ((s32[8,16,2]{0,2,1:T(2,128)}), s32[8,16,2]{0,2,1:T(2,128)S(1)}, u32[]{:S(2)}, u32[]{:S(2)}) async-start(s32[8,16,2]{0,2,1:T(2,128)} %copy.38), calls=%async_computation.1 | async-start | bytes 32768 | tf_op jit(solution)/shard_map/all_to_all | solution.py:104
  621.4 626.3 %all-to-all-start.3 = ((bf16[8,16,2,256,256]{4,3,2,0,1:T(8,128)(2,1)}), bf16[8,16,2,256,256]{4,3,2,0,1:T(8,128)(2,1)}, u32[]{:S(2)}, u32[]{:S(2)}) async-start(bf16[8,16,2,256,256]{4,3,2,0,1:T(8,128)(2,1)} %copy.42), calls=%async_computation.3 | async-start | bytes 67108864 | tf_op jit(solution)/shard_map/all_to_all | solution.py:97
  1345.6 30.5 %copy-start.1 = (f32[8,512]{1,0:T(8,128)S(1)}, f32[8,512]{1,0:T(8,128)}, u32[]{:S(2)}) copy-start(f32[8,512]{1,0:T(8,128)} %param.11) | copy-start | bytes 49156
where the time goes:
time: 1380 us
  waiting for transfers between devices  982 us (71%)
  local copies, waits for them, and re-layouts  237 us (17%)
  matrix products  107 us (8%)
  starting transfers between devices  27 us (2%)
  blocking collectives  21 us (2%)
    all_to_all x1, waiting for transfers between devices, on_device(): lax.all_to_all(lax.all_to_all(built_tiles, 'prow', split_axis=0, concat_a...  619 us
    all_to_all x1, waiting for transfers between devices, on_device(): lax.all_to_all(built_tiles, 'prow', split_axis=0, concat_axis=0, tiled=True)  364 us
    dynamic_update_slice x32, local copies, waits for them, and re-layouts, on_device(): lax.map(lambda slot_group: build_tiles(slot_group[0], slot_group[1], basi...  69.1 us
    unnamed x12, local copies, waits for them, and re-layouts  60.6 us
    dot_general x16, matrix products, build_tiles(): jnp.einsum('qa,gqb->gab', inner_rows, exchange_group, preferred_element_t...  52.9 us
    dot_general x1, local copies, waits for them, and re-layouts, sum_blocks(): jnp.dot(select, built_tiles.reshape(built_tiles.shape[0], spline_width *...  44 us
  transfers between devices with their start and end apart: 4, of which 2 were waited for; matrix products, arithmetic and copies ran while one was open for 16% of the time, Pallas kernels for 0%

commit v1 on v0

--- a/solution.py
+++ b/solution.py
@@ -6,6 +6,22 @@
 CAP = 2
 BAND = 2
 RBLK = 32
+
+
+def swapped_with_each(x, axis, split, join):
+    ways, here = (lax.axis_size(axis), lax.axis_index(axis))
+    width = x.shape[split] // ways
+    dims = list(x.shape)
+    dims[split] = width
+    height = dims[join]
+    dims[join] = height * ways
+    full = jnp.zeros(dims, x.dtype)
+    for mask in range(ways):
+        part = lax.dynamic_slice_in_dim(x, (here ^ mask) * width, width, axis=split)
+        if mask:
+            part = lax.ppermute(part, axis, [(d, d ^ mask) for d in range(ways)])
+        full = lax.dynamic_update_slice_in_dim(full, part, (here ^ mask) * height, axis=join)
+    return full
 
 
 def build_tiles(weights_group, exchange_group, basis):
@@ -94,12 +110,11 @@
     )
     built_tiles = built_tiles.reshape(row_devs, col_devs, CAP, spline_count, spline_count)
     received, idents = (
-        lax.all_to_all(
+        swapped_with_each(
             lax.all_to_all(built_tiles, "prow", split_axis=0, concat_axis=0, tiled=True),
             "pcol",
-            split_axis=1,
-            concat_axis=1,
-            tiled=True,
+            1,
+            1,
         ),
         lax.all_to_all(
             lax.all_to_all(

time: 1380 us -> 1250 us (0.906)
  waiting for transfers between devices: 982 us -> 721 us
  blocking collectives: 21 us -> 153 us
    all_to_all x3 -> x0, waiting for transfers between devices: 619 us -> none  [the longest x1 619 us: on_device(): lax.all_to_all(lax.all_to_all(built_tiles, 'prow', split_axis=0, concat_a...]
    ppermute x0 -> x15, waiting for transfers between devices: none -> 357 us  [swapped_with_each(): part = lax.ppermute(part, axis, [(d, d ^ mask) for d in range(ways)])]
    all_to_all x0 -> x2, blocking collectives: none -> 132 us  [the longest x1 124 us: on_device(): lax.all_to_all(lax.all_to_all(slot_ids.reshape(row_devs, col_devs, CAP),...]
    all_to_all x2 -> x0, local copies, waits for them, and re-layouts: 45.9 us -> none  [the longest x1 23 us: on_device(): lax.all_to_all(built_tiles, 'prow', split_axis=0, concat_axis=0, tiled=True)]
    reshape x0 -> x1, local copies, waits for them, and re-layouts: none -> 43.9 us  [on_device(): built_tiles.reshape(row_devs, col_devs, CAP, spline_count, spline_count)]
    dynamic_update_slice x32 -> x15, local copies, waits for them, and re-layouts: 69.1 us -> 31.3 us  [swapped_with_each(): lax.dynamic_update_slice_in_dim(full, part, (here ^ mask) * height, axis=...]
    ppermute x0 -> x15, starting transfers between devices: none -> 30.7 us  [swapped_with_each(): part = lax.ppermute(part, axis, [(d, d ^ mask) for d in range(ways)])]
    all_to_all x3 -> x0, starting transfers between devices: 19.8 us -> none  [the longest x1 8.27 us: on_device(): lax.all_to_all(lax.all_to_all(slot_ids.reshape(row_devs, col_devs, CAP),...]
  transfers between devices with their start and end apart: 4 -> 16, of which waited for: 2 -> 10; matrix products, arithmetic and copies ran while one was open for 16% -> 2% of each run, Pallas kernels for 0% -> 0%
where the time goes in v1:
time: 1250 us; the launch traced here: 1240 us
  waiting for transfers between devices  721 us (58%)
  local copies, waits for them, and re-layouts  224 us (18%)
  blocking collectives  153 us (12%)
  matrix products  107 us (9%)
  starting transfers between devices  37.8 us (3%)
    all_to_all x1, waiting for transfers between devices, on_device(): lax.all_to_all(built_tiles, 'prow', split_axis=0, concat_axis=0, tiled=True)  364 us
    ppermute x15, waiting for transfers between devices, swapped_with_each(): part = lax.ppermute(part, axis, [(d, d ^ mask) for d in range(ways)])  357 us
    all_to_all x1, blocking collectives, on_device(): lax.all_to_all(lax.all_to_all(slot_ids.reshape(row_devs, col_devs, CAP),...  124 us
    unnamed x44, local copies, waits for them, and re-layouts  60.7 us
    dot_general x16, matrix products, build_tiles(): jnp.einsum('qa,gqb->gab', inner_rows, exchange_group, preferred_element_t...  53.3 us
    dot_general x1, local copies, waits for them, and re-layouts, sum_blocks(): jnp.dot(select, built_tiles.reshape(built_tiles.shape[0], spline_width *...  43.9 us
    reshape x1, local copies, waits for them, and re-layouts, on_device(): built_tiles.reshape(row_devs, col_devs, CAP, spline_count, spline_count)  43.9 us
    dynamic_update_slice x15, local copies, waits for them, and re-layouts, swapped_with_each(): lax.dynamic_update_slice_in_dim(full, part, (here ^ mask) * height, axis=...  31.3 us
  transfers between devices with their start and end apart: 16, of which 10 were waited for; matrix products, arithmetic and copies ran while one was open for 2% of the time, Pallas kernels for 0%

profile of v1, /device:TPU:80, one launch (start us, length us, event | category | flops | bytes accessed | tf_op | source)
XLA Modules:
  0.0 1242.9 jit_solution(8863728128588895684)
XLA Ops:
  1.6 21.0 %all-gather = bf16[16,4,512]{2,1,0:T(4,128)(2,1)S(1)} all-gather(bf16[1,4,512]{2,1,0:T(4,128)(2,1)} %bitcast.71), channel_id=1, replica_groups=mesh['prow'=8,'pcol'=16] {'pcol'}, dimensions={0}, use_global_device_ids=true | all-gather | bytes 69632 | tf_op jit(solution)/shard_map/all_gather | solution.py:54
  22.6 13.9 %copy.38 = bf16[24,8,128,256]{3,1,2,0:T(8,128)(2,1)} copy(bf16[24,8,128,256]{3,2,1,0:T(8,128)(2,1)} %bitcast.62) | data formatting | bytes 25165824
  38.2 12.8 %convolution_convert_fusion = bf16[256,32768]{1,0:T(8,128)(2,1)} fusion(bf16[192,32768]{1,0:T(8,128)(2,1)} %bitcast.59, s32[192]{0:T(256)S(1)} %copy-done.18), kind=kOutput, calls=%fused_computation.13 | convolution fusion | flops 3229663232 | bytes 29360896 | tf_op jit(solution)/shard_map/dot_general | solution.py:97
  51.0 15.7 %copy.39 = bf16[32,8,128,256]{3,2,1,0:T(8,128)(2,1)} copy(bf16[32,8,128,256]{3,1,2,0:T(8,128)(2,1)} %bitcast.58) | data formatting | bytes 33554432
  66.7 76.1 %while.10 = (s32[]{:T(128)}, bf16[16,16,256,256]{2,3,1,0:T(8,128)(2,1)}, bf16[16,16,512]{2,1,0:T(8,128)(2,1)S(1)}, bf16[512,256]{1,0:T(8,128)(2,1)S(1)}, bf16[16,16,128,256]{3,2,1,0:T(8,128)(2,1)}, /*index=5*/s32[]{:T(128)}) while((s32[]{:T(128)}, bf16[16,16,256,256]{2,3,1,0:T(8,128)(2,1)}, bf16[16,16,512]{2,1,0:T(8,128)(2,1)S(1)}, ...), condition=%wide.region_4.5_spmd, body=%wide.region_3.4_spmd.sunk | while | flops 1348476928 | bytes 13288529 | solution.py:104
  142.8 43.9 %copy.32 = bf16[8,16,2,256,256]{4,3,2,1,0:T(8,128)(2,1)} copy(bf16[8,16,2,256,256]{3,4,2,1,0:T(8,128)(2,1)} %bitcast.60) | data formatting | bytes 67108864 | tf_op jit(solution)/shard_map/reshape | solution.py:111
  193.8 364.2 %all-to-all-done.2 = bf16[8,16,2,256,256]{4,3,2,1,0:T(8,128)(2,1)} async-done(((bf16[8,16,2,256,256]{4,3,2,1,0:T(8,128)(2,1)}), bf16[8,16,2,256,256]{4,3,2,1,0:T(8,128)(2,1)}, u32[]{:S(2)}, u32[]{:S(2)}) %all-to-all-start.2) | async-done | bytes 33554464 | tf_op jit(solution)/shard_map/all_to_all | solution.py:114
  558.0 10.9 broadcast_in_dim.55
  568.9 16.9 %constant_dynamic-slice_fusion.14 = (bf16[8,1,2,256,256]{4,3,2,1,0:T(8,128)(2,1)S(1)}, bf16[8,1,2,256,256]{4,3,2,1,0:T(8,128)(2,1)}, bf16[8,1,2,256,256]{4,3,2,1...) fusion(bf16[8,16,2,256,256]{4,3,2,1,0:T(8,128)(2,1)} %all-to-al, ...), kind=kLoop, calls=%fused_computation.68 | loop fusion | bytes 67108928 | tf_op jit(solution)/shard_map/dynamic_slice | solution.py:20
  597.4 40.9 %collective-permute-done.9 = bf16[8,1,2,256,256]{4,3,2,1,0:T(8,128)(2,1)S(1)} collective-permute-done((bf16[8,1,2,256,256]{4,3,2,1,0:T(8,128)(2,1)S(1)}, bf16[8,1,2,256,256]{4,3,2,1,0:T(8,128)(2,1)S(1)}, u32[]{:S(2)}, u32[]{:S(2)}) %collective-permute-start.9) | collective-permute-done | bytes 2097184 | tf_op jit(solution)/shard_map/ppermute | solution.py:22
  641.0 42.7 %collective-permute-done.8 = bf16[8,1,2,256,256]{4,3,2,1,0:T(8,128)(2,1)S(1)} collective-permute-done((bf16[8,1,2,256,256]{4,3,2,1,0:T(8,128)(2,1)S(1)}, bf16[8,1,2,256,256]{4,3,2,1,0:T(8,128)(2,1)S(1)}, u32[]{:S(2)}, u32[]{:S(2)}) %collective-permute-start.8) | collective-permute-done | bytes 2097184 | tf_op jit(solution)/shard_map/ppermute | solution.py:22
  684.5 42.8 %collective-permute-done.7 = bf16[8,1,2,256,256]{4,3,2,1,0:T(8,128)(2,1)S(1)} collective-permute-done((bf16[8,1,2,256,256]{4,3,2,1,0:T(8,128)(2,1)S(1)}, bf16[8,1,2,256,256]{4,3,2,1,0:T(8,128)(2,1)S(1)}, u32[]{:S(2)}, u32[]{:S(2)}) %collective-permute-start.7) | collective-permute-done | bytes 2097184 | tf_op jit(solution)/shard_map/ppermute | solution.py:22
  729.2 43.2 %collective-permute-done.6 = bf16[8,1,2,256,256]{4,3,2,1,0:T(8,128)(2,1)S(1)} collective-permute-done((bf16[8,1,2,256,256]{4,3,2,1,0:T(8,128)(2,1)S(1)}, bf16[8,1,2,256,256]{4,3,2,1,0:T(8,128)(2,1)S(1)}, u32[]{:S(2)}, u32[]{:S(2)}) %collective-permute-start.6) | collective-permute-done | bytes 2097184 | tf_op jit(solution)/shard_map/ppermute | solution.py:22
  775.2 43.4 %collective-permute-done.5 = bf16[8,1,2,256,256]{4,3,2,1,0:T(8,128)(2,1)S(1)} collective-permute-done((bf16[8,1,2,256,256]{4,3,2,1,0:T(8,128)(2,1)S(1)}, bf16[8,1,2,256,256]{4,3,2,1,0:T(8,128)(2,1)S(1)}, u32[]{:S(2)}, u32[]{:S(2)}) %collective-permute-start.5) | collective-permute-done | bytes 2097184 | tf_op jit(solution)/shard_map/ppermute | solution.py:22
  820.7 41.8 %collective-permute-done.4 = bf16[8,1,2,256,256]{4,3,2,1,0:T(8,128)(2,1)S(1)} collective-permute-done((bf16[8,1,2,256,256]{4,3,2,1,0:T(8,128)(2,1)S(1)}, bf16[8,1,2,256,256]{4,3,2,1,0:T(8,128)(2,1)S(1)}, u32[]{:S(2)}, u32[]{:S(2)}) %collective-permute-start.4) | collective-permute-done | bytes 2097184 | tf_op jit(solution)/shard_map/ppermute | solution.py:22
  865.0 42.5 %collective-permute-done.3 = bf16[8,1,2,256,256]{4,3,2,1,0:T(8,128)(2,1)S(1)} collective-permute-done((bf16[8,1,2,256,256]{4,3,2,1,0:T(8,128)(2,1)S(1)}, bf16[8,1,2,256,256]{4,3,2,1,0:T(8,128)(2,1)S(1)}, u32[]{:S(2)}, u32[]{:S(2)}) %collective-permute-start.3) | collective-permute-done | bytes 2097184 | tf_op jit(solution)/shard_map/ppermute | solution.py:22
  910.2 7.7 all_to_all.15
  917.9 124.1 %all_to_all.16 = s32[8,16,2]{0,2,1:T(2,128)S(1)} all-to-all(s32[8,16,2]{0,2,1:T(2,128)S(1)} %copy.29), channel_id=1, replica_groups=mesh['prow'=8,'pcol'=16] {'pcol'}, dimensions={1} | all-to-all | bytes 2048 | tf_op jit(solution)/shard_map/all_to_all | solution.py:119
  1075.2 18.9 %collective-permute-done.13 = bf16[8,1,2,256,256]{4,3,2,1,0:T(8,128)(2,1)S(1)} collective-permute-done((bf16[8,1,2,256,256]{4,3,2,1,0:T(8,128)(2,1)}, bf16[8,1,2,256,256]{4,3,2,1,0:T(8,128)(2,1)S(1)}, u32[]{:S(2)}, u32[]{:S(2)}) %collective-permute-start.13) | collective-permute-done | bytes 2097184 | tf_op jit(solution)/shard_map/ppermute | solution.py:22
  1095.4 40.6 %collective-permute-done.14 = bf16[8,1,2,256,256]{4,3,2,1,0:T(8,128)(2,1)S(1)} collective-permute-done((bf16[8,1,2,256,256]{4,3,2,1,0:T(8,128)(2,1)S(1)}, bf16[8,1,2,256,256]{4,3,2,1,0:T(8,128)(2,1)S(1)}, u32[]{:S(2)}, u32[]{:S(2)}) %collective-permute-start.14) | collective-permute-done | bytes 2097184 | tf_op jit(solution)/shard_map/ppermute | solution.py:22
  1137.4 31.0 %copy.40 = bf16[32,8,256,256]{3,1,2,0:T(8,128)(2,1)} copy(bf16[32,8,256,256]{3,2,1,0:T(8,128)(2,1)} %bitcast.55) | data formatting | bytes 67108864
  1168.4 43.9 %copy.35 = bf16[65536,256]{1,0:T(8,128)(2,1)} copy(bf16[65536,256]{0,1:T(8,128)(2,1)} %bitcast.57) | data formatting | bytes 67108864 | tf_op jit(solution)/shard_map/dot_general | solution.py:45
  1212.4 19.0 %convolution_convert_fusion.1 = bf16[64,256,256]{2,0,1:T(8,128)(2,1)} fusion(bf16[256,256,256]{2,1,0:T(8,128)(2,1)} %bitcast.56, s32[256]{0:T(256)S(1)} %eq.101), kind=kOutput, calls=%fused_computation.14 | convolution fusion | flops 2151694336 | bytes 41944064 | tf_op jit(solution)/shard_map/dot_general | solution.py:45
  1231.3 11.5 copy.36
  (173 shorter events, 149.0 us)
Async XLA Ops:
  0.0 37.3 %copy-start = (f32[8,512]{1,0:T(8,128)S(1)}, f32[8,512]{1,0:T(8,128)}, u32[]{:S(2)}) copy-start(f32[8,512]{1,0:T(8,128)} %param.11) | copy-start | bytes 49156
  186.6 371.4 %all-to-all-start.2 = ((bf16[8,16,2,256,256]{4,3,2,1,0:T(8,128)(2,1)}), bf16[8,16,2,256,256]{4,3,2,1,0:T(8,128)(2,1)}, u32[]{:S(2)}, u32[]{:S(2)}) async-start(bf16[8,16,2,256,256]{4,3,2,1,0:T(8,128)(2,1)} %copy.32), calls=%async_computation.2 | async-start | bytes 67108864 | tf_op jit(solution)/shard_map/all_to_all | solution.py:114
  585.8 52.5 %collective-permute-start.9 = (bf16[8,1,2,256,256]{4,3,2,1,0:T(8,128)(2,1)S(1)}, bf16[8,1,2,256,256]{4,3,2,1,0:T(8,128)(2,1)S(1)}, u32[]{:S(2)}, u32[]{:S(2)}) collective-permute-start(bf16[8,1,2,256,256]{4,3,2,1,0:T(8,128)(2,1)S(1)} %get-tuple-element.70), channel_id=1, source_target_pairs={{0,10},{1,11},{2,8},{3,9},{4,14},{5,15},{6,12},{7,13},{8,2},{9,3},... | collective-permute-start | bytes 6291464 | tf_op jit(solution)/shard_map/ppermute | solution.py:22
  589.4 94.3 %collective-permute-start.8 = (bf16[8,1,2,256,256]{4,3,2,1,0:T(8,128)(2,1)S(1)}, bf16[8,1,2,256,256]{4,3,2,1,0:T(8,128)(2,1)S(1)}, u32[]{:S(2)}, u32[]{:S(2)}) collective-permute-start(bf16[8,1,2,256,256]{4,3,2,1,0:T(8,128)(2,1)S(1)} %get-tuple-element.71), channel_id=1, source_target_pairs={{0,9},{1,8},{2,11},{3,10},{4,13},{5,12},{6,15},{7,14},{8,1},{9,0},... | collective-permute-start | bytes 6291464 | tf_op jit(solution)/shard_map/ppermute | solution.py:22
  592.3 135.1 %collective-permute-start.7 = (bf16[8,1,2,256,256]{4,3,2,1,0:T(8,128)(2,1)S(1)}, bf16[8,1,2,256,256]{4,3,2,1,0:T(8,128)(2,1)S(1)}, u32[]{:S(2)}, u32[]{:S(2)}) collective-permute-start(bf16[8,1,2,256,256]{4,3,2,1,0:T(8,128)(2,1)S(1)} %get-tuple-element.72), channel_id=1, source_target_pairs={{0,8},{1,9},{2,10},{3,11},{4,12},{5,13},{6,14},{7,15},{8,0},{9,1},... | collective-permute-start | bytes 6291464 | tf_op jit(solution)/shard_map/ppermute | solution.py:22
  594.3 178.0 %collective-permute-start.6 = (bf16[8,1,2,256,256]{4,3,2,1,0:T(8,128)(2,1)S(1)}, bf16[8,1,2,256,256]{4,3,2,1,0:T(8,128)(2,1)S(1)}, u32[]{:S(2)}, u32[]{:S(2)}) collective-permute-start(bf16[8,1,2,256,256]{4,3,2,1,0:T(8,128)(2,1)S(1)} %get-tuple-element.73), channel_id=1, source_target_pairs={{0,7},{1,6},{2,5},{3,4},{4,3},{5,2},{6,1},{7,0},{8,15},{9,14},{10,... | collective-permute-start | bytes 6291464 | tf_op jit(solution)/shard_map/ppermute | solution.py:22
  595.8 222.9 %collective-permute-start.5 = (bf16[8,1,2,256,256]{4,3,2,1,0:T(8,128)(2,1)S(1)}, bf16[8,1,2,256,256]{4,3,2,1,0:T(8,128)(2,1)S(1)}, u32[]{:S(2)}, u32[]{:S(2)}) collective-permute-start(bf16[8,1,2,256,256]{4,3,2,1,0:T(8,128)(2,1)S(1)} %get-tuple-element.74), channel_id=1, source_target_pairs={{0,6},{1,7},{2,4},{3,5},{4,2},{5,3},{6,0},{7,1},{8,14},{9,15},{10,... | collective-permute-start | bytes 6291464 | tf_op jit(solution)/shard_map/ppermute | solution.py:22
  638.3 269.9 %copy-start.3 = (bf16[8,1,2,256,256]{4,3,2,1,0:T(8,128)(2,1)}, bf16[8,1,2,256,256]{4,3,2,1,0:T(8,128)(2,1)S(1)}, u32[]{:S(2)}) copy-start(bf16[8,1,2,256,256]{4,3,2,1,0:T(8,128)(2,1)S(1)} %collective-permute-done.9) | copy-start | bytes 6291460
  638.3 224.2 %collective-permute-start.4 = (bf16[8,1,2,256,256]{4,3,2,1,0:T(8,128)(2,1)S(1)}, bf16[8,1,2,256,256]{4,3,2,1,0:T(8,128)(2,1)S(1)}, u32[]{:S(2)}, u32[]{:S(2)}) collective-permute-start(bf16[8,1,2,256,256]{4,3,2,1,0:T(8,128)(2,1)S(1)} %get-tuple-element.75), channel_id=1, source_target_pairs={{0,5},{1,4},{2,7},{3,6},{4,1},{5,0},{6,3},{7,2},{8,13},{9,12},{10,... | collective-permute-start | bytes 6291464 | tf_op jit(solution)/shard_map/ppermute | solution.py:22
  683.7 223.9 %copy-start.5 = (bf16[8,1,2,256,256]{4,3,2,1,0:T(8,128)(2,1)}, bf16[8,1,2,256,256]{4,3,2,1,0:T(8,128)(2,1)S(1)}, u32[]{:S(2)}) copy-start(bf16[8,1,2,256,256]{4,3,2,1,0:T(8,128)(2,1)S(1)} %collective-permute-done.8) | copy-start | bytes 6291460
  683.7 223.8 %collective-permute-start.3 = (bf16[8,1,2,256,256]{4,3,2,1,0:T(8,128)(2,1)S(1)}, bf16[8,1,2,256,256]{4,3,2,1,0:T(8,128)(2,1)S(1)}, u32[]{:S(2)}, u32[]{:S(2)}) collective-permute-start(bf16[8,1,2,256,256]{4,3,2,1,0:T(8,128)(2,1)S(1)} %get-tuple-element.76), channel_id=1, source_target_pairs={{0,4},{1,5},{2,6},{3,7},{4,0},{5,1},{6,2},{7,3},{8,12},{9,13},{10,... | collective-permute-start | bytes 6291464 | tf_op jit(solution)/shard_map/ppermute | solution.py:22
  727.3 180.3 %copy-start.7 = (bf16[8,1,2,256,256]{4,3,2,1,0:T(8,128)(2,1)}, bf16[8,1,2,256,256]{4,3,2,1,0:T(8,128)(2,1)S(1)}, u32[]{:S(2)}) copy-start(bf16[8,1,2,256,256]{4,3,2,1,0:T(8,128)(2,1)S(1)} %collective-permute-done.7) | copy-start | bytes 6291460
  727.3 180.9 %collective-permute-start.2 = (bf16[8,1,2,256,256]{4,3,2,1,0:T(8,128)(2,1)S(1)}, bf16[8,1,2,256,256]{4,3,2,1,0:T(8,128)(2,1)S(1)}, u32[]{:S(2)}, u32[]{:S(2)}) collective-permute-start(bf16[8,1,2,256,256]{4,3,2,1,0:T(8,128)(2,1)S(1)} %get-tuple-element.77), channel_id=1, source_target_pairs={{0,3},{1,2},{2,1},{3,0},{4,7},{5,6},{6,5},{7,4},{8,11},{9,10},{10,... | collective-permute-start | bytes 6291464 | tf_op jit(solution)/shard_map/ppermute | solution.py:22
  772.4 135.2 %copy-start.9 = (bf16[8,1,2,256,256]{4,3,2,1,0:T(8,128)(2,1)}, bf16[8,1,2,256,256]{4,3,2,1,0:T(8,128)(2,1)S(1)}, u32[]{:S(2)}) copy-start(bf16[8,1,2,256,256]{4,3,2,1,0:T(8,128)(2,1)S(1)} %collective-permute-done.6) | copy-start | bytes 6291460
  772.4 270.0 %collective-permute-start = (bf16[8,1,2,256,256]{4,3,2,1,0:T(8,128)(2,1)}, bf16[8,1,2,256,256]{4,3,2,1,0:T(8,128)(2,1)}, u32[]{:S(2)}, u32[]{:S(2)}) collective-permute-start(bf16[8,1,2,256,256]{4,3,2,1,0:T(8,128)(2,1)} %get-tuple-element.79), channel_id=1, source_target_pairs={{0,1},{1,0},{2,3},{3,2},{4,5},{5,4},{6,7},{7,6},{8,9},{9,8},{10,11... | collective-permute-start | bytes 6291464 | tf_op jit(solution)/shard_map/ppermute | solution.py:22
  818.7 88.9 %copy-start.11 = (bf16[8,1,2,256,256]{4,3,2,1,0:T(8,128)(2,1)}, bf16[8,1,2,256,256]{4,3,2,1,0:T(8,128)(2,1)S(1)}, u32[]{:S(2)}) copy-start(bf16[8,1,2,256,256]{4,3,2,1,0:T(8,128)(2,1)S(1)} %collective-permute-done.5) | copy-start | bytes 6291460
  818.7 229.7 %collective-permute-start.1 = (bf16[8,1,2,256,256]{4,3,2,1,0:T(8,128)(2,1)}, bf16[8,1,2,256,256]{4,3,2,1,0:T(8,128)(2,1)}, u32[]{:S(2)}, u32[]{:S(2)}) collective-permute-start(bf16[8,1,2,256,256]{4,3,2,1,0:T(8,128)(2,1)} %get-tuple-element.78), channel_id=1, source_target_pairs={{0,2},{1,3},{2,0},{3,1},{4,6},{5,7},{6,4},{7,5},{8,10},{9,11},{10,... | collective-permute-start | bytes 6291464 | tf_op jit(solution)/shard_map/ppermute | solution.py:22
  862.5 45.7 %copy-start.13 = (bf16[8,1,2,256,256]{4,3,2,1,0:T(8,128)(2,1)}, bf16[8,1,2,256,256]{4,3,2,1,0:T(8,128)(2,1)S(1)}, u32[]{:S(2)}) copy-start(bf16[8,1,2,256,256]{4,3,2,1,0:T(8,128)(2,1)S(1)} %collective-permute-done.4) | copy-start | bytes 6291460
  862.5 203.5 %collective-permute-start.10 = (bf16[8,1,2,256,256]{4,3,2,1,0:T(8,128)(2,1)}, bf16[8,1,2,256,256]{4,3,2,1,0:T(8,128)(2,1)}, u32[]{:S(2)}, u32[]{:S(2)}) collective-permute-start(bf16[8,1,2,256,256]{4,3,2,1,0:T(8,128)(2,1)} %get-tuple-element.69), channel_id=1, source_target_pairs={{0,11},{1,10},{2,9},{3,8},{4,15},{5,14},{6,13},{7,12},{8,3},{9,2},... | collective-permute-start | bytes 6291464 | tf_op jit(solution)/shard_map/ppermute | solution.py:22
  907.6 161.5 %collective-permute-start.11 = (bf16[8,1,2,256,256]{4,3,2,1,0:T(8,128)(2,1)}, bf16[8,1,2,256,256]{4,3,2,1,0:T(8,128)(2,1)}, u32[]{:S(2)}, u32[]{:S(2)}) collective-permute-start(bf16[8,1,2,256,256]{4,3,2,1,0:T(8,128)(2,1)} %get-tuple-element.68), channel_id=1, source_target_pairs={{0,12},{1,13},{2,14},{3,15},{4,8},{5,9},{6,10},{7,11},{8,4},{9,5},... | collective-permute-start | bytes 6291464 | tf_op jit(solution)/shard_map/ppermute | solution.py:22
  908.3 163.9 %collective-permute-start.12 = (bf16[8,1,2,256,256]{4,3,2,1,0:T(8,128)(2,1)}, bf16[8,1,2,256,256]{4,3,2,1,0:T(8,128)(2,1)}, u32[]{:S(2)}, u32[]{:S(2)}) collective-permute-start(bf16[8,1,2,256,256]{4,3,2,1,0:T(8,128)(2,1)} %get-tuple-element.67), channel_id=1, source_target_pairs={{0,13},{1,12},{2,15},{3,14},{4,9},{5,8},{6,11},{7,10},{8,5},{9,4},... | collective-permute-start | bytes 6291464 | tf_op jit(solution)/shard_map/ppermute | solution.py:22
  1042.4 51.7 %collective-permute-start.13 = (bf16[8,1,2,256,256]{4,3,2,1,0:T(8,128)(2,1)}, bf16[8,1,2,256,256]{4,3,2,1,0:T(8,128)(2,1)S(1)}, u32[]{:S(2)}, u32[]{:S(2)}) collective-permute-start(bf16[8,1,2,256,256]{4,3,2,1,0:T(8,128)(2,1)} %get-tuple-element.66), channel_id=1, source_target_pairs={{0,14},{1,15},{2,12},{3,13},{4,10},{5,11},{6,8},{7,9},{8,6},{9,7},... | collective-permute-start | bytes 6291464 | tf_op jit(solution)/shard_map/ppermute | solution.py:22
  1048.4 87.7 %collective-permute-start.14 = (bf16[8,1,2,256,256]{4,3,2,1,0:T(8,128)(2,1)S(1)}, bf16[8,1,2,256,256]{4,3,2,1,0:T(8,128)(2,1)S(1)}, u32[]{:S(2)}, u32[]{:S(2)}) collective-permute-start(bf16[8,1,2,256,256]{4,3,2,1,0:T(8,128)(2,1)S(1)} %get-tuple-element.65), channel_id=1, source_target_pairs={{0,15},{1,14},{2,13},{3,12},{4,11},{5,10},{6,9},{7,8},{8,7},{9,6},... | collective-permute-start | bytes 6291464 | tf_op jit(solution)/shard_map/ppermute | solution.py:22
  1212.4 30.5 %copy-start.1 = (f32[8,512]{1,0:T(8,128)S(1)}, f32[8,512]{1,0:T(8,128)}, u32[]{:S(2)}) copy-start(f32[8,512]{1,0:T(8,128)} %param.11) | copy-start | bytes 49156
  (12 other events, 141.7 us)
